TPU v7x, 128 devices: a whole 4x4x4 slice. The times are simulated.
128 devices in a mesh: dp: 16 (over x_lo, z, core), tensor: 8 (over y, x_hi).
Axes of the slice: x: 4 (x_hi: 2, x_lo: 2; x = x_hi * 2 + x_lo), y: 4, z: 4, core: 2. Of those that a mesh axis runs over, the one named last changes fastest.
Arguments:
- tokens: bfloat16 [12288, 1024], P('dp'), may hold values from -72 to 72
- w_qkv: float32 [1024, 3072], P(('dp', 'tensor')), may hold values from -0.1875 to 0.1875
- w_out: float32 [1024, 1024], P(None, ('dp', 'tensor')), may hold values from -0.1875 to 0.1875
- w_up: float32 [1024, 4096], P(('dp', 'tensor')), may hold values from -0.1875 to 0.1875
- w_down: float32 [4096, 1024], P(None, ('dp', 'tensor')), may hold values from -0.09375 to 0.09375
- slot_request: int32 [96, 128], replicated, may hold values from -1 to 3, as said below
Outputs:
- encoded: bfloat16 [12288, 1024], P('dp')
Inputs may be any that keep to these rules, and one draw needn't show every extreme that they name: `slot_request`: requests are numbered 0 to 3, all present; each request holds 1 to 48 pages and one holds exactly 48; each request's pages are full except its last page, whose empty slots are its final ones; pages may sit in any slot of the table.
All inputs are finite; a program needn't handle non-finite values.
Results may differ from a plain program's by a relative error of at most 0.025.
The roundings to bfloat16 on the way count: a program that leaves them out, or rounds other values in their place, can miss the bound.
Values may be sent and summed in bfloat16 or wider, within the bound.
No kernel may reach another device: no remote copies, remote signals or barrier semaphores. Data moves between devices by JAX's collectives and lax.ppermute only.
A program may use at most 128 MiB of HBM per device.

v0:
```python
import math
import jax
import jax.numpy as jnp
from jax import lax
from jax.sharding import PartitionSpec as P

D = 1024
H = 16


def layer_norm(value):
    mean = jnp.mean(value, axis=-1, keepdims=True)
    centred = value - mean
    spread = jnp.mean(centred * centred, axis=-1, keepdims=True)
    return centred * lax.rsqrt(spread + 1e-05)


def shards(tokens, w_qkv, w_out, w_up, w_down, slot_request):
    groups = lax.axis_size("tensor")
    tensor_rank = lax.axis_index("tensor")
    row_split = (w_qkv.astype(jnp.bfloat16), w_up.astype(jnp.bfloat16))
    col_split = (w_out.astype(jnp.bfloat16), w_down.astype(jnp.bfloat16))
    qkv_full, up_full = (
        lax.all_gather(row_split[0], ("dp", "tensor"), axis=0, tiled=True),
        lax.all_gather(row_split[1], ("dp", "tensor"), axis=0, tiled=True),
    )
    out_full, down_full = (
        lax.all_gather(col_split[0], ("dp", "tensor"), axis=1, tiled=True),
        lax.all_gather(col_split[1], ("dp", "tensor"), axis=1, tiled=True),
    )
    qkv_cols = qkv_full.shape[1] // groups
    up_cols = up_full.shape[1] // groups
    out_rows = out_full.shape[0] // groups
    down_rows = down_full.shape[0] // groups
    qkv_block = lax.dynamic_slice_in_dim(qkv_full, tensor_rank * qkv_cols, qkv_cols, 1)
    up_block = lax.dynamic_slice_in_dim(up_full, tensor_rank * up_cols, up_cols, 1)
    out_block = lax.dynamic_slice_in_dim(out_full, tensor_rank * out_rows, out_rows, 0)
    down_block = lax.dynamic_slice_in_dim(down_full, tensor_rank * down_rows, down_rows, 0)
    tok_rows = tokens.shape[0]
    head_size = D // H
    heads_here = qkv_block.shape[1] // (3 * head_size)
    qkv = jnp.dot(tokens, qkv_block, preferred_element_type=jnp.float32).astype(jnp.bfloat16)
    qkv = qkv.reshape(tok_rows, heads_here, 3, head_size)
    queries = qkv[:, :, 0, :]
    key_rows = qkv[:, :, 1, :].reshape(tok_rows, heads_here * head_size)
    value_rows = qkv[:, :, 2, :].reshape(tok_rows, heads_here * head_size)
    slot_ids = slot_request.reshape(-1)
    own_ids = lax.dynamic_slice_in_dim(slot_ids, lax.axis_index("dp") * tok_rows, tok_rows, 0)
    scale = 1.0 / math.sqrt(head_size)

    def update(carry, key_block, value_block, key_ids):
        running_max, total, accumulated = carry
        width = key_block.shape[0]
        key_heads = key_block.reshape(width, heads_here, head_size)
        value_heads = value_block.reshape(width, heads_here, head_size)
        scores = (
            jnp.einsum("qhd,khd->hqk", queries, key_heads, preferred_element_type=jnp.float32)
            * scale
        )
        allowed = (own_ids[:, None] == key_ids[None, :])[None]
        masked = jnp.where(allowed, scores, -1e30)
        new_max = jnp.maximum(running_max, jnp.max(masked, axis=-1))
        weights = jnp.where(allowed, jnp.exp(masked - new_max[..., None]), 0.0)
        rescale = jnp.exp(running_max - new_max)
        total = total * rescale + jnp.sum(weights, axis=-1)
        mixed = jnp.einsum(
            "hqk,khd->qhd",
            weights.astype(jnp.bfloat16),
            value_heads,
            preferred_element_type=jnp.float32,
        )
        accumulated = accumulated * jnp.transpose(rescale)[..., None] + mixed
        return (new_max, total, accumulated)

    def visit(carry, key_block, value_block, key_ids):
        return update(carry, key_block, value_block, key_ids)

    initial = (
        jnp.full((heads_here, tok_rows), -1e30, jnp.float32),
        jnp.zeros((heads_here, tok_rows), jnp.float32),
        jnp.zeros((tok_rows, heads_here, head_size), jnp.float32),
    )
    key_piece = lax.all_gather(key_rows, "dp", axis=0, tiled=True)
    value_piece = lax.all_gather(value_rows, "dp", axis=0, tiled=True)
    key_count = key_piece.shape[0]
    steps = key_count // tok_rows
    piece_ids = slot_ids.reshape(steps, tok_rows)
    key_steps = key_piece.reshape(steps, tok_rows, key_piece.shape[1])
    value_steps = value_piece.reshape(steps, tok_rows, value_piece.shape[1])

    def one_step(state, inputs):
        key_block, value_block, key_ids = inputs
        return (visit(state, key_block, value_block, key_ids), None)

    result, unused = lax.scan(one_step, initial, (key_steps, value_steps, piece_ids))
    running_max, total, accumulated = result
    attn = (
        (accumulated / jnp.transpose(total)[..., None])
        .astype(jnp.bfloat16)
        .reshape(tok_rows, heads_here * head_size)
    )
    proj = lax.psum(
        jnp.dot(attn, out_block, preferred_element_type=jnp.float32).astype(jnp.bfloat16), "tensor"
    ).astype(jnp.float32)
    first = layer_norm(tokens.astype(jnp.float32) + proj).astype(jnp.bfloat16)
    inner = jax.nn.gelu(
        jnp.dot(first, up_block, preferred_element_type=jnp.float32), approximate=False
    ).astype(jnp.bfloat16)
    ffn = lax.psum(
        jnp.dot(inner, down_block, preferred_element_type=jnp.float32).astype(jnp.bfloat16),
        "tensor",
    ).astype(jnp.float32)
    live = (own_ids >= 0).astype(jnp.float32)[:, None]
    encoded = (layer_norm(first.astype(jnp.float32) + ffn) * live).astype(jnp.bfloat16)
    return encoded


def solution(mesh):
    in_specs = (
        P("dp", None),
        P(("dp", "tensor"), None),
        P(None, ("dp", "tensor")),
        P(("dp", "tensor"), None),
        P(None, ("dp", "tensor")),
        P(),
    )
    out_specs = P("dp", None)
    return jax.shard_map(shards, mesh=mesh, in_specs=in_specs, out_specs=out_specs, check_vma=False)
```

profile of v0, /device:TPU:0, one launch (start us, length us, event | category | flops | bytes accessed | tf_op | source)
XLA Modules:
  0.0 1536.8 jit_solution(17673529418651723079)
XLA Ops:
  8.1 309.5 %all-gather.7.cloned.1.call-done = bf16[1024,3072]{1,0:T(8,128)(2,1)} async-done(((bf16[8,3072]{1,0:T(8,128)(2,1)}), bf16[1024,3072]{1,0:T(8,128)(2,1)}) %all-gather.7.cloned.1.call-update) | async-done | bytes 6291472 | tf_op jit(solution)/shard_map/all_gather | solution.py:24
  317.6 2.5 convolution_convert_fusion.2
  322.6 35.3 %all-gather.9.cloned.1.call-done = bf16[12288,128]{0,1:T(8,128)(2,1)} async-done(((bf16[768,128]{0,1:T(8,128)(2,1)}), bf16[12288,128]{0,1:T(8,128)(2,1)}) %all-gather.9.cloned.1.call-update) | async-done | bytes 3145744 | tf_op jit(solution)/shard_map/all_gather | solution.py:83
  357.8 4.7 copy.17
  362.5 32.4 %all-gather.11.cloned.1.call-done = bf16[12288,128]{0,1:T(8,128)(2,1)} async-done(((bf16[768,128]{0,1:T(8,128)(2,1)}), bf16[12288,128]{0,1:T(8,128)(2,1)}) %all-gather.11.cloned.1.call-update) | async-done | bytes 3145744 | tf_op jit(solution)/shard_map/all_gather | solution.py:84
  394.9 4.7 copy.20
  399.6 165.9 %while.15 = (s32[]{:T(128)}, f32[2,768]{1,0:T(2,128)S(1)}, f32[2,768]{1,0:T(2,128)S(1)}, f32[768,2,64]{0,2,1:T(8,128)S(1)}, s32[768]{0:T(1024)S(1)}, /*index=5*/...) while((s32[]{:T(128)}, f32[2,768]{1,0:T(2,128)S(1)}, ...), condition=%wide.region_3.4_spmd.clone, body=%wide.region_0.3_spmd.clone.sunk | while | flops 318219264 | bytes 33730736 | solution.py:95
  401.3 3.2 fusion.126
  404.6 4.0 fusion.130
  411.6 3.2 fusion.126
  415.0 4.0 fusion.130
  422.0 3.2 fusion.126
  425.4 4.0 fusion.130
  432.4 3.2 fusion.126
  435.7 4.0 fusion.130
  442.7 3.2 fusion.126
  446.1 4.0 fusion.130
  453.1 3.2 fusion.126
  456.5 4.0 fusion.130
  463.5 3.2 fusion.126
  466.8 4.0 fusion.130
  473.8 3.2 fusion.126
  477.2 4.0 fusion.130
  484.2 3.2 fusion.126
  487.6 4.0 fusion.130
  494.6 3.2 fusion.126
  497.9 4.0 fusion.130
  504.9 3.2 fusion.126
  508.3 4.0 fusion.130
  515.3 3.2 fusion.126
  518.7 4.0 fusion.130
  525.7 3.2 fusion.126
  529.0 4.0 fusion.130
  536.0 3.2 fusion.126
  539.4 4.0 fusion.130
  546.4 3.2 fusion.126
  549.8 4.0 fusion.130
  556.8 3.2 fusion.126
  560.2 4.0 fusion.130
  565.5 132.8 %all-gather.13.cloned.1.call-done = bf16[1024,1024]{0,1:T(8,128)(2,1)} async-done(((bf16[1024,8]{0,1:T(8,128)(2,1)}), bf16[1024,1024]{0,1:T(8,128)(2,1)}) %all-gather.13.cloned.1.call-update) | async-done | bytes 2097168 | tf_op jit(solution)/shard_map/all_gather | solution.py:28
  698.4 2.8 convolution_convert_fusion.1
  702.9 96.7 %all-reduce.3.cloned.1.call-done = bf16[768,1024]{1,0:T(8,128)(2,1)} async-done(((bf16[768,1024]{1,0:T(8,128)(2,1)}), bf16[768,1024]{1,0:T(8,128)(2,1)}) %all-reduce.3.cloned.1.call-update) | async-done | bytes 1572880 | tf_op jit(solution)/shard_map/psum | solution.py:102
  799.6 2.0 fusion.19
  803.0 305.4 %all-gather.15.cloned.1.call-done = bf16[1024,4096]{1,0:T(8,128)(2,1)} async-done(((bf16[8,4096]{1,0:T(8,128)(2,1)}), bf16[1024,4096]{1,0:T(8,128)(2,1)}) %all-gather.15.cloned.1.call-update) | async-done | bytes 8388624 | tf_op jit(solution)/shard_map/all_gather | solution.py:25
  1108.4 311.5 %all-gather.17.cloned.1.call-done = bf16[4096,1024]{0,1:T(8,128)(2,1)} async-done(((bf16[4096,8]{0,1:T(8,128)(2,1)}), bf16[4096,1024]{0,1:T(8,128)(2,1)}) %all-gather.17.cloned.1.call-update) | async-done | bytes 8388624 | tf_op jit(solution)/shard_map/all_gather | solution.py:29
  1419.9 7.6 convolution_convert_fusion
  1427.6 97.8 %all-reduce.5.cloned.1.call-done = bf16[768,1024]{1,0:T(8,128)(2,1)} async-done(((bf16[768,1024]{1,0:T(8,128)(2,1)}), bf16[768,1024]{1,0:T(8,128)(2,1)}) %all-reduce.5.cloned.1.call-update) | async-done | bytes 1572880 | tf_op jit(solution)/shard_map/psum | solution.py:109
  1525.4 2.0 fusion.21
  (273 shorter events, 58.4 us)
Async XLA Ops:
  6.5 311.1 %all-gather.7.cloned.1.call-start = ((), (), s32[]{:S(2)}) async-start(), calls=%async_computation | async-start | bytes 6340608 | tf_op jit(solution)/shard_map/all_gather | solution.py:24
  8.1 349.8 %all-gather.9.cloned.1.call-start = ((), (), s32[]{:S(2)}) async-start(), calls=%async_computation.1 | async-start | bytes 3342336 | tf_op jit(solution)/shard_map/all_gather | solution.py:83
  320.1 1.6 copy-start.6
  320.1 2.3 copy-start.5
  321.0 74.0 %all-gather.11.cloned.1.call-start = ((), (), s32[]{:S(2)}) async-start(), calls=%async_computation.2 | async-start | bytes 3342336 | tf_op jit(solution)/shard_map/all_gather | solution.py:84
  321.7 376.7 %all-gather.13.cloned.1.call-start = ((), (), s32[]{:S(2)}) async-start(), calls=%async_computation.3 | async-start | bytes 2113536 | tf_op jit(solution)/shard_map/all_gather | solution.py:28
  322.4 477.2 %all-reduce.3.cloned.1.call-start = ((), (), s32[]{:S(2)}) async-start(), calls=%async_computation.4 | async-start | bytes 3145728 | tf_op jit(solution)/shard_map/psum | solution.py:102
  404.5 4.2 slice-start
  404.6 4.1 slice-start.1
  414.8 4.2 slice-start
  415.0 4.1 slice-start.1
  425.2 4.2 slice-start
  425.4 4.1 slice-start.1
  435.6 4.2 slice-start
  435.7 4.1 slice-start.1
  445.9 4.2 slice-start
  446.1 4.1 slice-start.1
  456.3 4.2 slice-start
  456.5 4.1 slice-start.1
  466.7 4.2 slice-start
  466.8 4.1 slice-start.1
  477.0 4.2 slice-start
  477.2 4.1 slice-start.1
  487.4 4.2 slice-start
  487.6 4.1 slice-start.1
  497.8 4.2 slice-start
  497.9 4.1 slice-start.1
  508.1 4.2 slice-start
  508.3 4.1 slice-start.1
  518.5 4.2 slice-start
  518.7 4.1 slice-start.1
  528.9 4.2 slice-start
  529.0 4.1 slice-start.1
  539.2 4.2 slice-start
  539.4 4.1 slice-start.1
  549.6 4.2 slice-start
  549.8 4.1 slice-start.1
  560.0 4.2 slice-start
  560.1 4.1 slice-start.1
  698.4 2.9 copy-start.3
  698.4 3.6 copy-start.4
  698.4 101.2 %copy-start = (bf16[768,1024]{1,0:T(8,128)(2,1)S(1)}, bf16[768,1024]{1,0:T(8,128)(2,1)}, u32[]{:S(2)}) copy-start(bf16[768,1024]{1,0:T(8,128)(2,1)} %param.8) | copy-start | bytes 4718596
  701.2 407.2 %all-gather.15.cloned.1.call-start = ((), (), s32[]{:S(2)}) async-start(), calls=%async_computation.5 | async-start | bytes 8454144 | tf_op jit(solution)/shard_map/all_gather | solution.py:25
  701.9 718.0 %all-gather.17.cloned.1.call-start = ((), (), s32[]{:S(2)}) async-start(), calls=%async_computation.6 | async-start | bytes 8454144 | tf_op jit(solution)/shard_map/all_gather | solution.py:29
  702.7 822.7 %all-reduce.5.cloned.1.call-start = ((), (), s32[]{:S(2)}) async-start(), calls=%async_computation.7 | async-start | bytes 3145728 | tf_op jit(solution)/shard_map/psum | solution.py:109
  799.6 2.0 copy-start.1
  1525.4 2.0 copy-start.2
Sparse Core Ops, SparseCore 0:
  9.0 308.5 all-gather.6
  321.1 36.7 all-gather.8
  359.5 35.3 all-gather.10
  396.5 301.8 all-gather.12
  701.3 98.2 all-reduce.2
  801.1 307.2 all-gather.14
  1110.1 309.7 all-gather.16
  1427.7 97.5 all-reduce.4
where the time goes:
time: 1540 us
  waiting for transfers between devices  1320 us (86%)
  matrix products  128 us (8%)
  other arithmetic  38.2 us (2%)
  local copies, waits for them, and re-layouts  32.3 us (2%)
    all_gather x1, waiting for transfers between devices, shards(): lax.all_gather(col_split[1], ('dp', 'tensor'), axis=1, tiled=True)  312 us
    all_gather x1, waiting for transfers between devices, shards(): lax.all_gather(row_split[0], ('dp', 'tensor'), axis=0, tiled=True)  309 us
    all_gather x1, waiting for transfers between devices, shards(): lax.all_gather(row_split[1], ('dp', 'tensor'), axis=0, tiled=True)  305 us
    all_gather x1, waiting for transfers between devices, shards(): lax.all_gather(col_split[0], ('dp', 'tensor'), axis=1, tiled=True)  133 us
    psum x1, waiting for transfers between devices, shards(): lax.psum(jnp.dot(inner, down_block, preferred_element_type=jnp.float32).a...  97.8 us
    psum x1, waiting for transfers between devices, shards(): lax.psum(jnp.dot(attn, out_block, preferred_element_type=jnp.float32).ast...  96.7 us
    dot_general x16, matrix products, update(): jnp.einsum('hqk,khd->qhd', weights.astype(jnp.bfloat16), value_heads, pre...  64.5 us
    dot_general x16, matrix products, update(): jnp.einsum('qhd,khd->hqk', queries, key_heads, preferred_element_type=jnp...  50.9 us
  transfers between devices with their start and end apart: 8, of which 8 were waited for; matrix products, arithmetic and copies ran while one was open for 12% of the time, Pallas kernels for 0%

commit v1 on v0

--- a/solution.py
+++ b/solution.py
@@ -6,6 +6,10 @@
 
 D = 1024
 H = 16
+
+
+def _define_bars(own_rows):
+    return jnp.sum(lax.all_gather(own_rows, axis_name="tensor"), axis=0)
 
 
 def layer_norm(value):
@@ -106,9 +110,8 @@
     inner = jax.nn.gelu(
         jnp.dot(first, up_block, preferred_element_type=jnp.float32), approximate=False
     ).astype(jnp.bfloat16)
-    ffn = lax.psum(
-        jnp.dot(inner, down_block, preferred_element_type=jnp.float32).astype(jnp.bfloat16),
-        "tensor",
+    ffn = _define_bars(
+        jnp.dot(inner, down_block, preferred_element_type=jnp.float32).astype(jnp.bfloat16)
     ).astype(jnp.float32)
     live = (own_ids >= 0).astype(jnp.float32)[:, None]
     encoded = (layer_norm(first.astype(jnp.float32) + ffn) * live).astype(jnp.bfloat16)

time: 1540 us -> 1590 us (1.032)
  waiting for transfers between devices: 1320 us -> 1370 us
    all_gather x0 -> x1, waiting for transfers between devices: none -> 146 us  [_define_bars(): return jnp.sum(lax.all_gather(own_rows, axis_name='tensor'), axis=0)]
    psum x1 -> x0, waiting for transfers between devices: 97.8 us -> none  [shards(): lax.psum(jnp.dot(inner, down_block, preferred_element_type=jnp.float32).a...]
  transfers between devices with their start and end apart: 8 -> 8, of which waited for: 8 -> 8; matrix products, arithmetic and copies ran while one was open for 12% -> 11% of each run, Pallas kernels for 0% -> 0%
where the time goes in v1:
time: 1590 us
  waiting for transfers between devices  1370 us (86%)
  matrix products  128 us (8%)
  other arithmetic  45 us (3%)
  local copies, waits for them, and re-layouts  32.3 us (2%)
    all_gather x1, waiting for transfers between devices, shards(): lax.all_gather(col_split[1], ('dp', 'tensor'), axis=1, tiled=True)  312 us
    all_gather x1, waiting for transfers between devices, shards(): lax.all_gather(row_split[0], ('dp', 'tensor'), axis=0, tiled=True)  309 us
    all_gather x1, waiting for transfers between devices, shards(): lax.all_gather(row_split[1], ('dp', 'tensor'), axis=0, tiled=True)  305 us
    all_gather x1, waiting for transfers between devices, _define_bars(): return jnp.sum(lax.all_gather(own_rows, axis_name='tensor'), axis=0)  146 us
    all_gather x1, waiting for transfers between devices, shards(): lax.all_gather(col_split[0], ('dp', 'tensor'), axis=1, tiled=True)  132 us
    psum x1, waiting for transfers between devices, shards(): lax.psum(jnp.dot(attn, out_block, preferred_element_type=jnp.float32).ast...  96.3 us
    dot_general x16, matrix products, update(): jnp.einsum('hqk,khd->qhd', weights.astype(jnp.bfloat16), value_heads, pre...  64.5 us
    dot_general x16, matrix products, update(): jnp.einsum('qhd,khd->hqk', queries, key_heads, preferred_element_type=jnp...  50.9 us
  transfers between devices with their start and end apart: 8, of which 8 were waited for; matrix products, arithmetic and copies ran while one was open for 11% of the time, Pallas kernels for 0%

profile of v1, /device:TPU:0, one launch (start us, length us, event | category | flops | bytes accessed | tf_op | source)
XLA Modules:
  0.0 1590.7 jit_solution(2955156019106034959)
XLA Ops:
  8.1 309.5 %all-gather.9.cloned.1.call-done = bf16[1024,3072]{1,0:T(8,128)(2,1)} async-done(((bf16[8,3072]{1,0:T(8,128)(2,1)}), bf16[1024,3072]{1,0:T(8,128)(2,1)}) %all-gather.9.cloned.1.call-update) | async-done | bytes 6291472 | tf_op jit(solution)/shard_map/all_gather | solution.py:28
  317.6 2.5 convolution_convert_fusion.2
  322.6 35.3 %all-gather.11.cloned.1.call-done = bf16[12288,128]{0,1:T(8,128)(2,1)} async-done(((bf16[768,128]{0,1:T(8,128)(2,1)}), bf16[12288,128]{0,1:T(8,128)(2,1)}) %all-gather.11.cloned.1.call-update) | async-done | bytes 3145744 | tf_op jit(solution)/shard_map/all_gather | solution.py:87
  357.8 4.7 copy.17
  362.5 32.4 %all-gather.13.cloned.1.call-done = bf16[12288,128]{0,1:T(8,128)(2,1)} async-done(((bf16[768,128]{0,1:T(8,128)(2,1)}), bf16[12288,128]{0,1:T(8,128)(2,1)}) %all-gather.13.cloned.1.call-update) | async-done | bytes 3145744 | tf_op jit(solution)/shard_map/all_gather | solution.py:88
  394.9 4.7 copy.20
  399.7 165.9 %while.15 = (s32[]{:T(128)}, f32[2,768]{1,0:T(2,128)S(1)}, f32[2,768]{1,0:T(2,128)S(1)}, f32[768,2,64]{0,2,1:T(8,128)S(1)}, s32[768]{0:T(1024)S(1)}, /*index=5*/...) while((s32[]{:T(128)}, f32[2,768]{1,0:T(2,128)S(1)}, ...), condition=%wide.region_3.4_spmd.clone, body=%wide.region_0.3_spmd.clone.sunk | while | flops 318219264 | bytes 33730736 | solution.py:99
  401.3 3.2 fusion.126
  404.7 4.0 fusion.130
  411.7 3.2 fusion.126
  415.1 4.0 fusion.130
  422.0 3.2 fusion.126
  425.4 4.0 fusion.130
  432.4 3.2 fusion.126
  435.8 4.0 fusion.130
  442.8 3.2 fusion.126
  446.2 4.0 fusion.130
  453.1 3.2 fusion.126
  456.5 4.0 fusion.130
  463.5 3.2 fusion.126
  466.9 4.0 fusion.130
  473.9 3.2 fusion.126
  477.3 4.0 fusion.130
  484.3 3.2 fusion.126
  487.6 4.0 fusion.130
  494.6 3.2 fusion.126
  498.0 4.0 fusion.130
  505.0 3.2 fusion.126
  508.4 4.0 fusion.130
  515.4 3.2 fusion.126
  518.8 4.0 fusion.130
  525.8 3.2 fusion.126
  529.1 4.0 fusion.130
  536.1 3.2 fusion.126
  539.5 4.0 fusion.130
  546.5 3.2 fusion.126
  549.9 4.0 fusion.130
  556.9 3.2 fusion.126
  560.3 4.0 fusion.130
  565.6 132.3 %all-gather.15.cloned.1.call-done = bf16[1024,1024]{0,1:T(8,128)(2,1)} async-done(((bf16[1024,8]{0,1:T(8,128)(2,1)}), bf16[1024,1024]{0,1:T(8,128)(2,1)}) %all-gather.15.cloned.1.call-update) | async-done | bytes 2097168 | tf_op jit(solution)/shard_map/all_gather | solution.py:32
  697.9 2.8 convolution_convert_fusion.1
  702.5 96.3 %all-reduce.2.cloned.1.call-done = bf16[768,1024]{1,0:T(8,128)(2,1)} async-done(((bf16[768,1024]{1,0:T(8,128)(2,1)}), bf16[768,1024]{1,0:T(8,128)(2,1)}) %all-reduce.2.cloned.1.call-update) | async-done | bytes 1572880 | tf_op jit(solution)/shard_map/psum | solution.py:106
  798.8 2.0 fusion.19
  802.2 305.4 %all-gather.17.cloned.1.call-done = bf16[1024,4096]{1,0:T(8,128)(2,1)} async-done(((bf16[8,4096]{1,0:T(8,128)(2,1)}), bf16[1024,4096]{1,0:T(8,128)(2,1)}) %all-gather.17.cloned.1.call-update) | async-done | bytes 8388624 | tf_op jit(solution)/shard_map/all_gather | solution.py:29
  1107.6 311.5 %all-gather.19.cloned.1.call-done = bf16[4096,1024]{0,1:T(8,128)(2,1)} async-done(((bf16[4096,8]{0,1:T(8,128)(2,1)}), bf16[4096,1024]{0,1:T(8,128)(2,1)}) %all-gather.19.cloned.1.call-update) | async-done | bytes 8388624 | tf_op jit(solution)/shard_map/all_gather | solution.py:33
  1419.1 7.6 convolution_convert_fusion
  1426.8 145.6 %all-gather.21.cloned.1.call-done = bf16[6144,1024]{1,0:T(8,128)(2,1)} async-done(((bf16[768,1024]{1,0:T(8,128)(2,1)}), bf16[6144,1024]{1,0:T(8,128)(2,1)}) %all-gather.21.cloned.1.call-update) | async-done | bytes 12582928 | tf_op jit(solution)/shard_map/all_gather | solution.py:12
  1572.4 8.4 reduce_sum.59
  (272 shorter events, 58.9 us)
Async XLA Ops:
  6.5 311.1 %all-gather.9.cloned.1.call-start = ((), (), s32[]{:S(2)}) async-start(), calls=%async_computation | async-start | bytes 6340608 | tf_op jit(solution)/shard_map/all_gather | solution.py:28
  8.1 349.8 %all-gather.11.cloned.1.call-start = ((), (), s32[]{:S(2)}) async-start(), calls=%async_computation.1 | async-start | bytes 3342336 | tf_op jit(solution)/shard_map/all_gather | solution.py:87
  320.1 1.6 copy-start.5
  320.1 2.3 copy-start.4
  321.0 74.0 %all-gather.13.cloned.1.call-start = ((), (), s32[]{:S(2)}) async-start(), calls=%async_computation.2 | async-start | bytes 3342336 | tf_op jit(solution)/shard_map/all_gather | solution.py:88
  321.7 376.2 %all-gather.15.cloned.1.call-start = ((), (), s32[]{:S(2)}) async-start(), calls=%async_computation.3 | async-start | bytes 2113536 | tf_op jit(solution)/shard_map/all_gather | solution.py:32
  322.4 476.4 %all-reduce.2.cloned.1.call-start = ((), (), s32[]{:S(2)}) async-start(), calls=%async_computation.4 | async-start | bytes 3145728 | tf_op jit(solution)/shard_map/psum | solution.py:106
  404.5 4.2 slice-start
  404.7 4.1 slice-start.1
  414.9 4.2 slice-start
  415.0 4.1 slice-start.1
  425.3 4.2 slice-start
  425.4 4.1 slice-start.1
  435.6 4.2 slice-start
  435.8 4.1 slice-start.1
  446.0 4.2 slice-start
  446.1 4.1 slice-start.1
  456.4 4.2 slice-start
  456.5 4.1 slice-start.1
  466.7 4.2 slice-start
  466.9 4.1 slice-start.1
  477.1 4.2 slice-start
  477.2 4.1 slice-start.1
  487.5 4.2 slice-start
  487.6 4.1 slice-start.1
  497.8 4.2 slice-start
  498.0 4.1 slice-start.1
  508.2 4.2 slice-start
  508.4 4.1 slice-start.1
  518.6 4.2 slice-start
  518.7 4.1 slice-start.1
  529.0 4.2 slice-start
  529.1 4.1 slice-start.1
  539.3 4.2 slice-start
  539.5 4.1 slice-start.1
  549.7 4.2 slice-start
  549.9 4.1 slice-start.1
  560.1 4.2 slice-start
  560.2 4.1 slice-start.1
  697.9 2.9 copy-start.2
  697.9 3.6 copy-start.3
  697.9 100.9 %copy-start = (bf16[768,1024]{1,0:T(8,128)(2,1)S(1)}, bf16[768,1024]{1,0:T(8,128)(2,1)}, u32[]{:S(2)}) copy-start(bf16[768,1024]{1,0:T(8,128)(2,1)} %param.8) | copy-start | bytes 4718596
  700.8 406.8 %all-gather.17.cloned.1.call-start = ((), (), s32[]{:S(2)}) async-start(), calls=%async_computation.5 | async-start | bytes 8454144 | tf_op jit(solution)/shard_map/all_gather | solution.py:29
  701.5 717.6 %all-gather.19.cloned.1.call-start = ((), (), s32[]{:S(2)}) async-start(), calls=%async_computation.6 | async-start | bytes 8454144 | tf_op jit(solution)/shard_map/all_gather | solution.py:33
  702.3 870.1 %all-gather.21.cloned.1.call-start = ((), (), s32[]{:S(2)}) async-start(), calls=%async_computation.7 | async-start | bytes 14155776 | tf_op jit(solution)/shard_map/all_gather | solution.py:12
  798.8 2.0 copy-start.1
Sparse Core Ops, SparseCore 0:
  9.0 308.5 all-gather.8
  321.1 36.7 all-gather.10
  359.5 35.3 all-gather.12
  396.5 301.4 all-gather.14
  700.9 97.8 all-reduce.1
  800.3 307.2 all-gather.16
  1109.3 309.7 all-gather.18
  1426.9 145.4 all-gather.20
